TPU v7x, 128 devices: a whole 4x4x4 slice. The times are simulated.
128 devices in a mesh: enc: 16 (over z, y), dp: 2 (over x_hi), tensor: 4 (over x_lo, core).
Axes of the slice: x: 4 (x_hi: 2, x_lo: 2; x = x_hi * 2 + x_lo), y: 4, z: 4, core: 2. Of those that a mesh axis runs over, the one named last changes fastest.
Arguments:
- hidden_in: bfloat16 [3, 64, 4096], P(None, 'dp', 'enc')
- self_cache: bfloat16 [64, 8, 2, 2048], P(('dp', 'enc'), None, None, 'tensor'), may hold values from -6 to 6
- src_pool: bfloat16 [64, 24, 2, 2048], P(('dp', 'enc'), None, None, 'tensor'), may hold values from -6 to 6
- assign: int32 [64], replicated, may hold values from 0 to 63, as said below
- src_len: int32 [64], replicated, may hold values from 1 to 24, 768 in all
- positions: int32 [64], replicated, may hold values from 1 to 8, 256 in all
- gain_self: float32 [4096], P('enc'), may hold values from 0.1 to 1.9
- w_qkv: bfloat16 [4096, 3, 2048], P('enc', None, 'tensor'), may hold values from -0.09375 to 0.09375
- w_out_self: bfloat16 [2048, 4096], P('tensor', 'enc'), may hold values from -0.125 to 0.125
- gain_cross: float32 [4096], P('enc'), may hold values from 0.1 to 1.9
- w_q_cross: bfloat16 [4096, 2048], P('enc', 'tensor'), may hold values from -0.09375 to 0.09375
- w_out_cross: bfloat16 [2048, 4096], P('tensor', 'enc'), may hold values from -0.125 to 0.125
Outputs:
- layer_out: bfloat16 [3, 64, 4096], P(None, 'dp', 'enc')
Inputs may be any that keep to these rules, and one draw needn't show every extreme that they name: `assign`: a permutation of the 64 sources; with blocks of 2 consecutive sequences or sources numbered d * 16 + e, the 2 sequences of block d * 16 + e read exactly one source from each block d2 * 16 + e that has the same e.
All inputs are finite; a program needn't handle non-finite values.
Results may differ from a plain program's by a relative error of at most 0.008.
Values may be sent and summed in bfloat16 or wider, within the bound.
No kernel may reach another device: no remote copies, remote signals or barrier semaphores. Data moves between devices by JAX's collectives and lax.ppermute only.
A program may use at most 64 MiB of HBM per device.

v0:
```python
import math
import jax
import jax.numpy as jnp
from jax import lax
from jax.sharding import PartitionSpec as P

D = 4096
DK = 256
STEPS = 3
EPSILON = 1e-06


def row_norm(rows_in, gain_vec):
    squares = lax.psum(jnp.sum(rows_in * rows_in, axis=1), "enc")
    return (rows_in * lax.rsqrt(squares / D + EPSILON)[:, None] * gain_vec[None, :]).astype(
        jnp.bfloat16
    )


def score_weight(scores):
    return jnp.exp(scores).astype(jnp.bfloat16)


def attend(query_rows, key_rows, value_rows, usable):
    count = query_rows.shape[0]
    head_count = query_rows.shape[1] // DK
    query_heads = query_rows.reshape(count, head_count, DK)
    key_heads = key_rows.reshape(count, key_rows.shape[1], head_count, DK)
    value_heads = value_rows.reshape(count, value_rows.shape[1], head_count, DK)
    scores = jnp.einsum(
        "nhd,nlhd->nhl", query_heads, key_heads, preferred_element_type=jnp.float32
    ) * (1.0 / math.sqrt(DK))
    weights = jnp.where(usable[:, None, :], score_weight(scores), jnp.zeros((), jnp.bfloat16))
    weighted = jnp.einsum("nhl,nlhd->nhd", weights, value_heads, preferred_element_type=jnp.float32)
    return (weighted, jnp.sum(weights.astype(jnp.float32), axis=-1))


def combine_heads(context, weight_out):
    partial_out = jnp.dot(context, weight_out, preferred_element_type=jnp.float32)
    return lax.psum(partial_out, "tensor")


def on_device(
    hidden_in,
    self_cache,
    src_pool,
    assign,
    src_len,
    positions,
    gain_self,
    w_qkv,
    w_out_self,
    gain_cross,
    w_q_cross,
    w_out_cross,
):
    dp_count = lax.axis_size("dp")
    enc_count = lax.axis_size("enc")
    seq_dev = self_cache.shape[0]
    per_pair = seq_dev // dp_count
    cache_len = self_cache.shape[1]
    source_len = src_pool.shape[1]
    enc_at = lax.axis_index("enc")
    dp_at = lax.axis_index("dp")
    block_at = dp_at * enc_count + enc_at
    slot_index = jnp.arange(seq_dev, dtype=jnp.int32)
    my_slots = block_at * seq_dev + slot_index
    my_positions = jnp.take(positions, my_slots)
    my_sources = jnp.take(assign, my_slots)
    place_at = jnp.arange(cache_len, dtype=jnp.int32)
    cache_usable = place_at[None, :] < my_positions[:, None]
    token_at = jnp.arange(source_len, dtype=jnp.int32)
    assign_view = assign.reshape(dp_count, enc_count, seq_dev)
    assign_grid = jnp.take(assign_view, enc_at, axis=1)
    owners = assign_grid // (seq_dev * enc_count)
    earlier = (owners[:, None, :] == owners[:, :, None]) & (
        slot_index[None, None, :] < slot_index[None, :, None]
    )
    slot_rank = jnp.sum(earlier.astype(jnp.int32), axis=2)
    recv_rows = jnp.take(owners, dp_at, axis=0) * per_pair + jnp.take(slot_rank, dp_at, axis=0)
    picked = (owners == dp_at)[:, :, None] & (
        slot_rank[:, :, None] == jnp.arange(per_pair, dtype=jnp.int32)[None, None, :]
    )
    chosen = jnp.sum(jnp.where(picked, (assign_grid % seq_dev)[:, :, None], 0), axis=1)
    chosen_flat = chosen.reshape(-1)
    outgoing = jnp.take(src_pool, chosen_flat, axis=0)
    arrived = lax.all_to_all(outgoing, "dp", split_axis=0, concat_axis=0, tiled=True)
    cross_kv = jnp.take(arrived, recv_rows, axis=0)
    cross_usable = token_at[None, :] < jnp.take(src_len, my_sources)[:, None]
    key_list = []
    value_list = []
    results = []
    for step_at in range(STEPS):
        current = hidden_in[step_at].astype(jnp.float32)
        normed = row_norm(current, gain_self)
        projected = jnp.einsum("sd,dcw->scw", normed, w_qkv, preferred_element_type=jnp.float32)
        own_proj = lax.psum_scatter(projected, "enc", scatter_dimension=0, tiled=True).astype(
            jnp.bfloat16
        )
        query_rows = own_proj[:, 0]
        key_list.append(own_proj[:, 1])
        value_list.append(own_proj[:, 2])
        weighted, totals = attend(
            query_rows, self_cache[:, :, 0], self_cache[:, :, 1], cache_usable
        )
        head_count = weighted.shape[1]
        query_heads = query_rows.astype(jnp.float32).reshape(seq_dev, head_count, DK)
        for key_new, value_new in zip(key_list, value_list):
            scores = jnp.sum(
                query_heads * key_new.astype(jnp.float32).reshape(seq_dev, head_count, DK), axis=-1
            ) * (1.0 / math.sqrt(DK))
            weights = score_weight(scores).astype(jnp.float32)
            weighted = weighted + weights[:, :, None] * value_new.astype(jnp.float32).reshape(
                seq_dev, head_count, DK
            )
            totals = totals + weights
        context = (
            (weighted / totals[:, :, None]).reshape(seq_dev, head_count * DK).astype(jnp.bfloat16)
        )
        context_all = lax.all_gather(context, "enc", axis=0, tiled=True)
        residual = current + combine_heads(context_all, w_out_self)
        normed_cross = row_norm(residual, gain_cross)
        cross_query = jnp.dot(normed_cross, w_q_cross, preferred_element_type=jnp.float32)
        own_query = lax.psum_scatter(cross_query, "enc", scatter_dimension=0, tiled=True).astype(
            jnp.bfloat16
        )
        weighted, totals = attend(own_query, cross_kv[:, :, 0], cross_kv[:, :, 1], cross_usable)
        context = (
            (weighted / totals[:, :, None]).reshape(seq_dev, head_count * DK).astype(jnp.bfloat16)
        )
        context_all = lax.all_gather(context, "enc", axis=0, tiled=True)
        output_rows = residual + combine_heads(context_all, w_out_cross)
        results.append(output_rows.astype(jnp.bfloat16))
    return jnp.stack(results)


def solution(mesh):
    in_specs = (
        P(None, "dp", "enc"),
        P(("dp", "enc"), None, None, "tensor"),
        P(("dp", "enc"), None, None, "tensor"),
        P(),
        P(),
        P(),
        P("enc"),
        P("enc", None, "tensor"),
        P("tensor", "enc"),
        P("enc"),
        P("enc", "tensor"),
        P("tensor", "enc"),
    )
    out_specs = P(None, "dp", "enc")
    return jax.shard_map(
        on_device, mesh=mesh, in_specs=in_specs, out_specs=out_specs, check_vma=False
    )
```

profile of v0, /device:TPU:1, one launch (start us, length us, event | category | flops | bytes accessed | tf_op | source)
XLA Modules:
  0.0 470.3 jit_solution(5215867503166297110)
XLA Ops:
  6.6 0.7 copy-done.1
  7.4 0.2 fusion.80
  7.8 0.6 gather_fusion.1
  8.5 0.2 copy-done.12
  8.7 0.7 gather_fusion.3
  9.4 0.8 broadcast_select_fusion.1
  10.2 5.0 %all-to-all-start = ((bf16[2,24,2,512]{3,2,1,0:T(2,128)(2,1)}), bf16[2,24,2,512]{3,2,1,0:T(2,128)(2,1)S(1)}, u32[]{:S(2)}, u32[]{:S(2)}) async-start(bf16[2,24,2,512]{3,2,1,0:T(2,128)(2,1)} %broadcast_select_fusion.1), calls=%async_computation | async-start | bytes 196608 | tf_op jit(solution)/shard_map/all_to_all | solution.py:87
  15.3 34.7 %all-reduce.9 = (f32[32]{0:T(128)S(1)}, f32[32]{0:T(128)S(1)}, f32[32]{0:T(128)S(1)}) all-reduce(f32[32]{0:T(128)S(1)} %get-tuple-element.35, f32[32]{0:T(128)S(1)} %get-tuple-element.36, f32[32]{0:T(128)S(1)} %get-tuple-element.37), channel_id=1, replica_groups=mesh['enc'=16,'dp'=2,'tensor'=4] {'enc'}, use_global_device_ids=true, to_apply=%region_1.3 | all-reduce | flops 96 | bytes 768 | tf_op jit(solution)/shard_map/psum | solution.py:14
  50.0 0.7 copy-done.14
  50.7 0.3 fusion.34
  51.0 0.3 fusion.37
  51.3 0.3 fusion.40
  51.6 0.7 copy-done.15
  52.2 0.6 dynamic-slice.11
  53.5 62.2 %all-reduce.20 = (bf16[32,3,512]{2,0,1:T(8,128)(2,1)S(1)}, bf16[32,3,512]{2,0,1:T(8,128)(2,1)S(1)}, bf16[32,3,512]{2,0,1:T(8,128)(2,1)S(1)}) all-reduce(f32[32,3,512]{2,0,1:T(8,128)S(1)} %fusion.40, f32[32,3,512]{2,0,1:T(8,128)S(1)} %fusion.34, f32[32,3,512]{2,0,1:T(8,128)S(1)} %fusion.37), channel_id=2, replica_groups=mesh['enc'=16,'dp'=2,'tensor'=4] {'enc'}, use_global_device_ids=true, to_apply=%region_2.4.clone | all-reduce | flops 147456 | bytes 884736
  116.0 0.6 copy-done.11
  117.1 0.4 copy-done.2
  117.5 0.6 gather_fusion
  119.0 15.2 %all-gather = bf16[16,2,512]{2,1,0:T(2,128)(2,1)S(1)} all-gather(bf16[1,2,512]{2,1,0:T(2,128)(2,1)S(1)} %reshape.380), channel_id=1, replica_groups=mesh['enc'=16,'dp'=2,'tensor'=4] {'enc'}, dimensions={0}, use_global_device_ids=true | all-gather | bytes 34816 | tf_op jit(solution)/shard_map/all_gather | solution.py:120
  134.2 18.0 %all-gather.2 = bf16[16,2,512]{2,1,0:T(2,128)(2,1)S(1)} all-gather(bf16[1,2,512]{2,1,0:T(2,128)(2,1)S(1)} %reshape.384), channel_id=1, replica_groups=mesh['enc'=16,'dp'=2,'tensor'=4] {'enc'}, dimensions={0}, use_global_device_ids=true | all-gather | bytes 34816 | tf_op jit(solution)/shard_map/all_gather | solution.py:120
  152.3 0.8 fusion.102
  153.1 0.8 fusion.105
  153.8 15.4 %all-gather.4 = bf16[16,2,512]{2,1,0:T(2,128)(2,1)S(1)} all-gather(bf16[1,2,512]{2,1,0:T(2,128)(2,1)S(1)} %reshape.388), channel_id=1, replica_groups=mesh['enc'=16,'dp'=2,'tensor'=4] {'enc'}, dimensions={0}, use_global_device_ids=true | all-gather | bytes 34816 | tf_op jit(solution)/shard_map/all_gather | solution.py:120
  169.3 0.8 fusion.108
  170.1 0.5 copy-done.3
  170.7 0.6 gather_fusion.2
  171.4 0.7 gather_fusion.4
  172.2 0.2 broadcast_select_fusion
  172.3 0.4 slice_reduce_fusion.1
  172.8 70.9 %all-reduce.19.cloned.1.call-done = (f32[32,256]{1,0:T(8,128)}, f32[32,256]{1,0:T(8,128)}, f32[32,256]{1,0:T(8,128)}) async-done(((f32[32,256]{1,0:T(8,128)}, f32[32,256]{1,0:T(8,128)}, f32[32,256]{1,0:T(8,128)}), (f32[32,256]{1,0:T(8,128)}, f32[32,256]{1,0:T(8,128)}, f32[32,256]{1,0:T(8,128)})) %all-reduce.19.cloned.1.call-update) | async-done | bytes 98320 | tf_op jit(solution)/shard_map/psum | solution.py:40
  243.7 1.0 multiply_reduce_fusion.2
  244.6 33.3 %all-reduce.7 = (f32[32]{0:T(128)S(1)}, f32[32]{0:T(128)S(1)}, f32[32]{0:T(128)S(1)}) all-reduce(f32[32]{0:T(128)S(1)} %get-tuple-element.34, f32[32]{0:T(128)S(1)} %get-tuple-element.33, f32[32]{0:T(128)S(1)} %get-tuple-element.32), channel_id=1, replica_groups=mesh['enc'=16,'dp'=2,'tensor'=4] {'enc'}, use_global_device_ids=true, to_apply=%region_34.38 | all-reduce | flops 96 | bytes 768 | tf_op jit(solution)/shard_map/psum | solution.py:14
  278.0 0.7 copy-done.13
  278.7 0.2 fusion.27
  278.9 0.6 copy-done.9
  279.4 0.2 fusion.29
  279.6 0.6 copy-done.10
  280.2 0.2 fusion.31
  280.4 57.3 %all-reduce.21 = (bf16[32,512]{1,0:T(8,128)(2,1)S(1)}, bf16[32,512]{1,0:T(8,128)(2,1)S(1)}, bf16[32,512]{1,0:T(8,128)(2,1)S(1)}) all-reduce(f32[32,512]{1,0:T(8,128)S(1)} %fusion.31, f32[32,512]{1,0:T(8,128)S(1)} %fusion.29, f32[32,512]{1,0:T(8,128)S(1)} %fusion.27), channel_id=7, replica_groups=mesh['enc'=16,'dp'=2,'tensor'=4] {'enc'}, use_global_device_ids=true, to_apply=%region_35.39.clone | all-reduce | flops 49152 | bytes 294912
  338.5 16.3 %all-gather.1 = bf16[16,2,512]{2,1,0:T(2,128)(2,1)S(1)} all-gather(bf16[1,2,512]{2,1,0:T(2,128)(2,1)S(1)} %reshape.382), channel_id=1, replica_groups=mesh['enc'=16,'dp'=2,'tensor'=4] {'enc'}, dimensions={0}, use_global_device_ids=true | all-gather | bytes 34816 | tf_op jit(solution)/shard_map/all_gather | solution.py:131
  355.0 17.4 %all-gather.3 = bf16[16,2,512]{2,1,0:T(2,128)(2,1)S(1)} all-gather(bf16[1,2,512]{2,1,0:T(2,128)(2,1)S(1)} %reshape.386), channel_id=1, replica_groups=mesh['enc'=16,'dp'=2,'tensor'=4] {'enc'}, dimensions={0}, use_global_device_ids=true | all-gather | bytes 34816 | tf_op jit(solution)/shard_map/all_gather | solution.py:131
  372.5 0.8 fusion.103
  373.2 0.8 fusion.106
  374.2 15.7 %all-gather.5 = bf16[16,2,512]{2,1,0:T(2,128)(2,1)S(1)} all-gather(bf16[1,2,512]{2,1,0:T(2,128)(2,1)S(1)} %reshape.390), channel_id=1, replica_groups=mesh['enc'=16,'dp'=2,'tensor'=4] {'enc'}, dimensions={0}, use_global_device_ids=true | all-gather | bytes 34816 | tf_op jit(solution)/shard_map/all_gather | solution.py:131
  389.9 0.8 fusion.109
  390.7 71.3 %all-reduce.17.cloned.1.call-done = (f32[32,256]{1,0:T(8,128)}, f32[32,256]{1,0:T(8,128)}, f32[32,256]{1,0:T(8,128)}) async-done(((f32[32,256]{1,0:T(8,128)}, f32[32,256]{1,0:T(8,128)}, f32[32,256]{1,0:T(8,128)}), (f32[32,256]{1,0:T(8,128)}, f32[32,256]{1,0:T(8,128)}, f32[32,256]{1,0:T(8,128)})) %all-reduce.17.cloned.1.call-update) | async-done | bytes 98320 | tf_op jit(solution)/shard_map/psum | solution.py:40
  462.1 0.8 fusion.28
  462.9 0.6 pad_maximum_fusion
  (109 shorter events, 3.5 us)
Async XLA Ops:
  6.5 43.5 %copy-start = (bf16[256,3,512]{2,0,1:T(8,128)(2,1)S(1)}, bf16[256,3,512]{2,0,1:T(8,128)(2,1)}, u32[]{:S(2)}) copy-start(bf16[256,3,512]{2,0,1:T(8,128)(2,1)} %param.25) | copy-start | bytes 2359300
  6.6 0.7 copy-start.1
  7.8 0.9 copy-start.12
  10.2 5.0 %copy-start.7 = (bf16[3,32,256]{2,1,0:T(8,128)(2,1)S(1)}, bf16[3,32,256]{2,1,0:T(8,128)(2,1)}, u32[]{:S(2)}) copy-start(bf16[3,32,256]{2,1,0:T(8,128)(2,1)} %param.18) | copy-start | bytes 147460
  10.2 161.2 %all-to-all-start = ((bf16[2,24,2,512]{3,2,1,0:T(2,128)(2,1)}), bf16[2,24,2,512]{3,2,1,0:T(2,128)(2,1)S(1)}, u32[]{:S(2)}, u32[]{:S(2)}) async-start(bf16[2,24,2,512]{3,2,1,0:T(2,128)(2,1)} %broadcast_select_fusion.1), calls=%async_computation | async-start | bytes 196608 | tf_op jit(solution)/shard_map/all_to_all | solution.py:87
  15.2 228.5 %all-reduce.19.cloned.1.call-start = ((), (), s32[]{:S(2)}) async-start(), calls=%async_computation.2 | async-start | bytes 196608 | tf_op jit(solution)/shard_map/psum | solution.py:40
  50.0 0.7 copy-start.14
  51.6 0.7 copy-start.15
  115.8 0.8 copy-start.11
  116.9 0.7 copy-start.2
  118.2 34.1 %copy-start.4 = (bf16[512,256]{1,0:T(8,128)(2,1)S(1)}, bf16[512,256]{1,0:T(8,128)(2,1)}, u32[]{:S(2)}) copy-start(bf16[512,256]{1,0:T(8,128)(2,1)} %param.26) | copy-start | bytes 786436
  170.0 0.7 copy-start.3
  170.0 292.0 %all-reduce.17.cloned.1.call-start = ((), (), s32[]{:S(2)}) async-start(), calls=%async_computation.1 | async-start | bytes 196608 | tf_op jit(solution)/shard_map/psum | solution.py:40
  172.3 105.7 %copy-start.6 = (bf16[256,512]{1,0:T(8,128)(2,1)S(1)}, bf16[256,512]{1,0:T(8,128)(2,1)}, u32[]{:S(2)}) copy-start(bf16[256,512]{1,0:T(8,128)(2,1)} %param.28) | copy-start | bytes 786436
  243.7 34.4 %copy-start.8 = (f32[32,256]{1,0:T(8,128)S(1)}, f32[32,256]{1,0:T(8,128)}, u32[]{:S(2)}) copy-start(f32[32,256]{1,0:T(8,128)} %get-tuple-element.64) | copy-start | bytes 98308
  278.0 0.7 copy-start.13
  278.7 0.8 copy-start.9
  279.4 0.8 copy-start.10
  337.9 34.6 %copy-start.5 = (bf16[512,256]{1,0:T(8,128)(2,1)S(1)}, bf16[512,256]{1,0:T(8,128)(2,1)}, u32[]{:S(2)}) copy-start(bf16[512,256]{1,0:T(8,128)(2,1)} %param.29) | copy-start | bytes 786436
Sparse Core Ops, SparseCore 0:
  170.2 73.4 all-reduce.18
  390.8 71.1 all-reduce.16
where the time goes:
time: 471 us; the launch traced here: 470 us
  blocking collectives  286 us (61%)
  waiting for transfers between devices  142 us (30%)
  between operations  14.4 us (3%)
  local copies, waits for them, and re-layouts  10.8 us (2%)
  matrix products  7.41 us (2%)
  starting transfers between devices  5 us (1%)
  other arithmetic  4.79 us (1%)
    psum x2, waiting for transfers between devices, combine_heads(): return lax.psum(partial_out, 'tensor')  142 us
    unnamed x2, blocking collectives  120 us
    all_gather x6, blocking collectives, on_device(): context_all = lax.all_gather(context, 'enc', axis=0, tiled=True)  98 us
    psum x2, blocking collectives, row_norm(): squares = lax.psum(jnp.sum(rows_in * rows_in, axis=1), 'enc')  68.1 us
  transfers between devices with their start and end apart: 3, of which 2 were waited for; matrix products, arithmetic and copies ran while one was open for 2% of the time, Pallas kernels for 0%

commit v1 on v0

--- a/solution.py
+++ b/solution.py
@@ -128,7 +128,9 @@
         context = (
             (weighted / totals[:, :, None]).reshape(seq_dev, head_count * DK).astype(jnp.bfloat16)
         )
-        context_all = lax.all_gather(context, "enc", axis=0, tiled=True)
+        context_all = jnp.concatenate(
+            lax.all_to_all(jnp.stack([context] * lax.axis_size("enc")), "enc", 0, 0), 0
+        )
         output_rows = residual + combine_heads(context_all, w_out_cross)
         results.append(output_rows.astype(jnp.bfloat16))
     return jnp.stack(results)

time: 471 us -> 438 us (0.930)
  blocking collectives: 286 us -> 236 us
  starting transfers between devices: 5 us -> 15.5 us
    all_gather x6 -> x3, blocking collectives: 98 us -> 48.6 us  [on_device(): context_all = lax.all_gather(context, 'enc', axis=0, tiled=True)]
    all_to_all x0 -> x3, waiting for transfers between devices: none -> 17.1 us  [on_device(): lax.all_to_all(jnp.stack([context] * lax.axis_size('enc')), 'enc', 0, 0)]
    psum x2, waiting for transfers between devices: 142 us -> 129 us  [combine_heads(): return lax.psum(partial_out, 'tensor')]
    all_to_all x0 -> x3, starting transfers between devices: none -> 10.5 us  [on_device(): lax.all_to_all(jnp.stack([context] * lax.axis_size('enc')), 'enc', 0, 0)]
  transfers between devices with their start and end apart: 3 -> 6, of which waited for: 2 -> 5; matrix products, arithmetic and copies ran while one was open for 2% -> 2% of each run, Pallas kernels for 0% -> 0%
where the time goes in v1:
time: 438 us; the launch traced here: 437 us
  blocking collectives  236 us (54%)
  waiting for transfers between devices  146 us (33%)
  starting transfers between devices  15.5 us (4%)
  between operations  14.5 us (3%)
  local copies, waits for them, and re-layouts  12.7 us (3%)
  matrix products  7.41 us (2%)
  other arithmetic  4.79 us (1%)
    psum x2, waiting for transfers between devices, combine_heads(): return lax.psum(partial_out, 'tensor')  129 us
    unnamed x2, blocking collectives  120 us
    psum x2, blocking collectives, row_norm(): squares = lax.psum(jnp.sum(rows_in * rows_in, axis=1), 'enc')  68.1 us
    all_gather x3, blocking collectives, on_device(): context_all = lax.all_gather(context, 'enc', axis=0, tiled=True)  48.6 us
    all_to_all x3, waiting for transfers between devices, on_device(): lax.all_to_all(jnp.stack([context] * lax.axis_size('enc')), 'enc', 0, 0)  17.1 us
    all_to_all x3, starting transfers between devices, on_device(): lax.all_to_all(jnp.stack([context] * lax.axis_size('enc')), 'enc', 0, 0)  10.5 us
  transfers between devices with their start and end apart: 6, of which 5 were waited for; matrix products, arithmetic and copies ran while one was open for 2% of the time, Pallas kernels for 0%

profile of v1, /device:TPU:1, one launch (start us, length us, event | category | flops | bytes accessed | tf_op | source)
XLA Modules:
  0.0 437.0 jit_solution(14208301053967108881)
XLA Ops:
  6.6 0.7 copy-done.1
  7.8 0.6 gather_fusion.1
  8.7 0.7 gather_fusion.3
  9.4 0.8 broadcast_select_fusion.1
  10.2 5.0 %all-to-all-start = ((bf16[2,24,2,512]{3,2,1,0:T(2,128)(2,1)}), bf16[2,24,2,512]{3,2,1,0:T(2,128)(2,1)S(1)}, u32[]{:S(2)}, u32[]{:S(2)}) async-start(bf16[2,24,2,512]{3,2,1,0:T(2,128)(2,1)} %broadcast_select_fusion.1), calls=%async_computation | async-start | bytes 196608 | tf_op jit(solution)/shard_map/all_to_all | solution.py:87
  15.3 34.7 %all-reduce.9 = (f32[32]{0:T(128)S(1)}, f32[32]{0:T(128)S(1)}, f32[32]{0:T(128)S(1)}) all-reduce(f32[32]{0:T(128)S(1)} %get-tuple-element.35, f32[32]{0:T(128)S(1)} %get-tuple-element.36, f32[32]{0:T(128)S(1)} %get-tuple-element.37), channel_id=1, replica_groups=mesh['enc'=16,'dp'=2,'tensor'=4] {'enc'}, use_global_device_ids=true, to_apply=%region_1.3 | all-reduce | flops 96 | bytes 768 | tf_op jit(solution)/shard_map/psum | solution.py:14
  50.0 0.7 copy-done.14
  50.7 0.3 fusion.34
  51.0 0.3 fusion.37
  51.3 0.3 fusion.40
  51.6 0.7 copy-done.15
  52.2 0.6 dynamic-slice.11
  53.5 62.2 %all-reduce.20 = (bf16[32,3,512]{2,0,1:T(8,128)(2,1)S(1)}, bf16[32,3,512]{2,0,1:T(8,128)(2,1)S(1)}, bf16[32,3,512]{2,0,1:T(8,128)(2,1)S(1)}) all-reduce(f32[32,3,512]{2,0,1:T(8,128)S(1)} %fusion.40, f32[32,3,512]{2,0,1:T(8,128)S(1)} %fusion.34, f32[32,3,512]{2,0,1:T(8,128)S(1)} %fusion.37), channel_id=2, replica_groups=mesh['enc'=16,'dp'=2,'tensor'=4] {'enc'}, use_global_device_ids=true, to_apply=%region_2.4.clone | all-reduce | flops 147456 | bytes 884736
  116.0 0.6 copy-done.11
  117.1 0.4 copy-done.2
  117.5 0.6 gather_fusion
  119.0 15.2 %all-gather = bf16[16,2,512]{2,1,0:T(2,128)(2,1)S(1)} all-gather(bf16[1,2,512]{2,1,0:T(2,128)(2,1)S(1)} %reshape.401), channel_id=1, replica_groups=mesh['enc'=16,'dp'=2,'tensor'=4] {'enc'}, dimensions={0}, use_global_device_ids=true | all-gather | bytes 34816 | tf_op jit(solution)/shard_map/all_gather | solution.py:120
  134.2 18.0 %all-gather.1 = bf16[16,2,512]{2,1,0:T(2,128)(2,1)S(1)} all-gather(bf16[1,2,512]{2,1,0:T(2,128)(2,1)S(1)} %reshape.403), channel_id=1, replica_groups=mesh['enc'=16,'dp'=2,'tensor'=4] {'enc'}, dimensions={0}, use_global_device_ids=true | all-gather | bytes 34816 | tf_op jit(solution)/shard_map/all_gather | solution.py:120
  152.3 0.8 fusion.105
  153.1 0.8 fusion.108
  153.8 15.4 %all-gather.2 = bf16[16,2,512]{2,1,0:T(2,128)(2,1)S(1)} all-gather(bf16[1,2,512]{2,1,0:T(2,128)(2,1)S(1)} %reshape.405), channel_id=1, replica_groups=mesh['enc'=16,'dp'=2,'tensor'=4] {'enc'}, dimensions={0}, use_global_device_ids=true | all-gather | bytes 34816 | tf_op jit(solution)/shard_map/all_gather | solution.py:120
  169.3 0.8 fusion.111
  170.1 0.6 copy-done.3
  170.7 0.6 gather_fusion.2
  171.4 0.7 gather_fusion.4
  172.3 0.4 slice_reduce_fusion
  172.7 70.9 %all-reduce.19.cloned.1.call-done = (f32[32,256]{1,0:T(8,128)}, f32[32,256]{1,0:T(8,128)}, f32[32,256]{1,0:T(8,128)}) async-done(((f32[32,256]{1,0:T(8,128)}, f32[32,256]{1,0:T(8,128)}, f32[32,256]{1,0:T(8,128)}), (f32[32,256]{1,0:T(8,128)}, f32[32,256]{1,0:T(8,128)}, f32[32,256]{1,0:T(8,128)})) %all-reduce.19.cloned.1.call-update) | async-done | bytes 98320 | tf_op jit(solution)/shard_map/psum | solution.py:40
  243.7 1.0 multiply_reduce_fusion.2
  244.6 33.3 %all-reduce.7 = (f32[32]{0:T(128)S(1)}, f32[32]{0:T(128)S(1)}, f32[32]{0:T(128)S(1)}) all-reduce(f32[32]{0:T(128)S(1)} %get-tuple-element.34, f32[32]{0:T(128)S(1)} %get-tuple-element.33, f32[32]{0:T(128)S(1)} %get-tuple-element.32), channel_id=1, replica_groups=mesh['enc'=16,'dp'=2,'tensor'=4] {'enc'}, use_global_device_ids=true, to_apply=%region_34.38 | all-reduce | flops 96 | bytes 768 | tf_op jit(solution)/shard_map/psum | solution.py:14
  278.0 0.7 copy-done.13
  278.9 0.6 copy-done.9
  279.6 0.6 copy-done.10
  280.4 57.3 %all-reduce.21 = (bf16[32,512]{1,0:T(8,128)(2,1)S(1)}, bf16[32,512]{1,0:T(8,128)(2,1)S(1)}, bf16[32,512]{1,0:T(8,128)(2,1)S(1)}) all-reduce(f32[32,512]{1,0:T(8,128)S(1)} %fusion.31, f32[32,512]{1,0:T(8,128)S(1)} %fusion.29, f32[32,512]{1,0:T(8,128)S(1)} %fusion.27), channel_id=7, replica_groups=mesh['enc'=16,'dp'=2,'tensor'=4] {'enc'}, use_global_device_ids=true, to_apply=%region_35.39.clone | all-reduce | flops 49152 | bytes 294912
  338.5 0.6 stack.14
  339.1 3.5 all-to-all-start.1
  343.1 6.0 %all-to-all-done.1 = bf16[16,2,512]{2,1,0:T(2,128)(2,1)S(1)} async-done(((bf16[16,2,512]{2,1,0:T(2,128)(2,1)}), bf16[16,2,512]{2,1,0:T(2,128)(2,1)S(1)}, u32[]{:S(2)}, u32[]{:S(2)}) %all-to-all-start.1) | async-done | bytes 32800 | tf_op jit(solution)/shard_map/all_to_all | solution.py:132
  349.0 0.6 stack.16
  349.7 3.5 all-to-all-start.2
  353.2 0.8 fusion.106
  354.0 5.6 %all-to-all-done.2 = bf16[16,2,512]{2,1,0:T(2,128)(2,1)S(1)} async-done(((bf16[16,2,512]{2,1,0:T(2,128)(2,1)}), bf16[16,2,512]{2,1,0:T(2,128)(2,1)S(1)}, u32[]{:S(2)}, u32[]{:S(2)}) %all-to-all-start.2) | async-done | bytes 32800 | tf_op jit(solution)/shard_map/all_to_all | solution.py:132
  359.6 0.6 stack.18
  360.2 3.5 all-to-all-start.3
  363.8 0.8 fusion.109
  364.5 5.6 %all-to-all-done.3 = bf16[16,2,512]{2,1,0:T(2,128)(2,1)S(1)} async-done(((bf16[16,2,512]{2,1,0:T(2,128)(2,1)}), bf16[16,2,512]{2,1,0:T(2,128)(2,1)S(1)}, u32[]{:S(2)}, u32[]{:S(2)}) %all-to-all-start.3) | async-done | bytes 32800 | tf_op jit(solution)/shard_map/all_to_all | solution.py:132
  370.1 0.8 fusion.112
  370.9 57.8 %all-reduce.17.cloned.1.call-done = (f32[32,256]{1,0:T(8,128)}, f32[32,256]{1,0:T(8,128)}, f32[32,256]{1,0:T(8,128)}) async-done(((f32[32,256]{1,0:T(8,128)}, f32[32,256]{1,0:T(8,128)}, f32[32,256]{1,0:T(8,128)}), (f32[32,256]{1,0:T(8,128)}, f32[32,256]{1,0:T(8,128)}, f32[32,256]{1,0:T(8,128)})) %all-reduce.17.cloned.1.call-update) | async-done | bytes 98320 | tf_op jit(solution)/shard_map/psum | solution.py:40
  428.7 0.8 fusion.28
  429.5 0.6 pad_maximum_fusion
  (115 shorter events, 4.6 us)
Async XLA Ops:
  6.5 43.5 %copy-start = (bf16[256,3,512]{2,0,1:T(8,128)(2,1)S(1)}, bf16[256,3,512]{2,0,1:T(8,128)(2,1)}, u32[]{:S(2)}) copy-start(bf16[256,3,512]{2,0,1:T(8,128)(2,1)} %param.25) | copy-start | bytes 2359300
  6.6 0.7 copy-start.1
  7.8 0.9 copy-start.12
  10.2 5.0 %copy-start.7 = (bf16[3,32,256]{2,1,0:T(8,128)(2,1)S(1)}, bf16[3,32,256]{2,1,0:T(8,128)(2,1)}, u32[]{:S(2)}) copy-start(bf16[3,32,256]{2,1,0:T(8,128)(2,1)} %param.18) | copy-start | bytes 147460
  10.2 161.2 %all-to-all-start = ((bf16[2,24,2,512]{3,2,1,0:T(2,128)(2,1)}), bf16[2,24,2,512]{3,2,1,0:T(2,128)(2,1)S(1)}, u32[]{:S(2)}, u32[]{:S(2)}) async-start(bf16[2,24,2,512]{3,2,1,0:T(2,128)(2,1)} %broadcast_select_fusion.1), calls=%async_computation | async-start | bytes 196608 | tf_op jit(solution)/shard_map/all_to_all | solution.py:87
  15.2 228.5 %all-reduce.19.cloned.1.call-start = ((), (), s32[]{:S(2)}) async-start(), calls=%async_computation.5 | async-start | bytes 196608 | tf_op jit(solution)/shard_map/psum | solution.py:40
  50.0 0.7 copy-start.14
  51.6 0.7 copy-start.15
  115.8 0.8 copy-start.11
  116.9 0.7 copy-start.2
  118.2 34.1 %copy-start.4 = (bf16[512,256]{1,0:T(8,128)(2,1)S(1)}, bf16[512,256]{1,0:T(8,128)(2,1)}, u32[]{:S(2)}) copy-start(bf16[512,256]{1,0:T(8,128)(2,1)} %param.26) | copy-start | bytes 786436
  170.0 0.7 copy-start.3
  172.3 105.7 %copy-start.6 = (bf16[256,512]{1,0:T(8,128)(2,1)S(1)}, bf16[256,512]{1,0:T(8,128)(2,1)}, u32[]{:S(2)}) copy-start(bf16[256,512]{1,0:T(8,128)(2,1)} %param.28) | copy-start | bytes 786436
  243.7 34.4 %copy-start.8 = (f32[32,256]{1,0:T(8,128)S(1)}, f32[32,256]{1,0:T(8,128)}, u32[]{:S(2)}) copy-start(f32[32,256]{1,0:T(8,128)} %get-tuple-element.64) | copy-start | bytes 98308
  278.0 0.7 copy-start.13
  278.7 0.8 copy-start.9
  279.4 0.8 copy-start.10
  338.2 15.0 %copy-start.5 = (bf16[512,256]{1,0:T(8,128)(2,1)S(1)}, bf16[512,256]{1,0:T(8,128)(2,1)}, u32[]{:S(2)}) copy-start(bf16[512,256]{1,0:T(8,128)(2,1)} %param.29) | copy-start | bytes 786436
  339.1 9.9 %all-to-all-start.1 = ((bf16[16,2,512]{2,1,0:T(2,128)(2,1)}), bf16[16,2,512]{2,1,0:T(2,128)(2,1)S(1)}, u32[]{:S(2)}, u32[]{:S(2)}) async-start(bf16[16,2,512]{2,1,0:T(2,128)(2,1)} %stack.14), calls=%async_computation.1 | async-start | bytes 65536 | tf_op jit(solution)/shard_map/all_to_all | solution.py:132
  349.7 9.9 %all-to-all-start.2 = ((bf16[16,2,512]{2,1,0:T(2,128)(2,1)}), bf16[16,2,512]{2,1,0:T(2,128)(2,1)S(1)}, u32[]{:S(2)}, u32[]{:S(2)}) async-start(bf16[16,2,512]{2,1,0:T(2,128)(2,1)} %stack.16), calls=%async_computation.2 | async-start | bytes 65536 | tf_op jit(solution)/shard_map/all_to_all | solution.py:132
  360.2 9.9 %all-to-all-start.3 = ((bf16[16,2,512]{2,1,0:T(2,128)(2,1)}), bf16[16,2,512]{2,1,0:T(2,128)(2,1)S(1)}, u32[]{:S(2)}, u32[]{:S(2)}) async-start(bf16[16,2,512]{2,1,0:T(2,128)(2,1)} %stack.18), calls=%async_computation.3 | async-start | bytes 65536 | tf_op jit(solution)/shard_map/all_to_all | solution.py:132
  363.7 65.0 %all-reduce.17.cloned.1.call-start = ((), (), s32[]{:S(2)}) async-start(), calls=%async_computation.4 | async-start | bytes 196608 | tf_op jit(solution)/shard_map/psum | solution.py:40
Sparse Core Ops, SparseCore 0:
  170.2 73.4 all-reduce.18
  371.0 57.6 all-reduce.16
